TPU v7x, 32 devices: a whole 2x2x4 slice. The times are simulated.
32 devices in a mesh: grp: 2 (over y), cell: 8 (over z, x), gene: 2 (over core).
Axes of the slice: x: 2, y: 2, z: 4, core: 2. Of those that a mesh axis runs over, the one named last changes fastest.
Arguments:
- expression: bfloat16 [2048, 16384], P(('grp', 'cell'), 'gene'), parts along dimension 0, may hold values from -6 to 6
- design: bfloat16 [2048, 128], P(('grp', 'cell')), parts along dimension 0, may hold values from -24 to 24
- quantile_level: float32 [16384], P('gene'), may hold values from 0.1 to 0.9
Outputs:
- quantile_slack: bfloat16 [2048, 16384], P(('grp', 'cell'), 'gene'), parts along dimension 0
- low_rank_coef: float32 [32768, 128], P(('grp', 'gene', 'cell')), parts along dimension 0
There are 2 independent parts, one for each index of `grp`. A program takes and returns all parts, laid end to end along the dimension named above; an argument that names none is the same for every part. Nothing has to cross between parts.
All inputs are finite; a program needn't handle non-finite values.
Results may differ from a plain program's by a relative error of at most 0.0025.
The roundings to bfloat16 on the way count: a program that leaves them out, or rounds other values in their place, can miss the bound.
Values may be sent and summed in bfloat16 or wider, within the bound.
No kernel may reach another device: no remote copies, remote signals or barrier semaphores. Data moves between devices by JAX's collectives and lax.ppermute only.
A program may use at most 64 MiB of HBM per device.

v0:
```python
import math
import jax
import jax.numpy as jnp
from jax import lax
from jax.sharding import PartitionSpec as P

NS_STEPS = 8
shrink_rate = 0.25


def matmul(left, right):
    return jnp.dot(left, right, precision=lax.Precision.HIGHEST)


def invert(matrix):
    identity = jnp.eye(matrix.shape[0], dtype=jnp.float32)
    factor = jnp.linalg.cholesky(matrix)
    lower_inv = lax.linalg.triangular_solve(factor, identity, left_side=True, lower=True)
    return matmul(lower_inv.T, lower_inv)


def newton(moment):
    identity = jnp.eye(moment.shape[0], dtype=jnp.float32)
    current = moment / jnp.trace(moment)
    root_inv = identity
    for sweep in range(NS_STEPS):
        middle = 1.5 * identity - 0.5 * matmul(root_inv, current)
        current = matmul(current, middle)
        root_inv = matmul(middle, root_inv)
    return root_inv


def per_device(expression, design, quantile_level):
    width = design.shape[1]
    identity = jnp.eye(width, dtype=jnp.float32)
    local_gram = lax.dot_general(
        design, design, (((0,), (0,)), ((), ())), preferred_element_type=jnp.float32
    )
    crossed = lax.psum_scatter(
        lax.dot_general(
            expression, design, (((0,), (0,)), ((), ())), preferred_element_type=jnp.float32
        ),
        "cell",
        scatter_dimension=0,
        tiled=True,
    )
    gram_total = lax.psum(local_gram, "cell")
    inverse = invert(gram_total + identity)
    coef = matmul(crossed, inverse)
    local_moment = lax.dot_general(
        coef, coef, (((0,), (0,)), ((), ())), precision=lax.Precision.HIGHEST
    )
    moment = lax.psum(local_moment, ("cell", "gene"))
    root_inv = newton(moment)
    low_rank_coef = coef - shrink_rate / math.sqrt(width) * matmul(coef, root_inv)
    coef_low = coef.astype(jnp.bfloat16)
    fitted = lax.dot_general(
        design,
        lax.all_gather(coef_low, "cell", axis=0, tiled=True),
        (((1,), (1,)), ((), ())),
        preferred_element_type=jnp.float32,
    )
    slack = expression.astype(jnp.float32) - fitted
    level = quantile_level[None, :]
    quantile_slack = (slack - jnp.clip(slack, level - 1.0, level)).astype(jnp.bfloat16)
    return (quantile_slack, low_rank_coef)


def solution(mesh):
    placed = (P(("grp", "cell"), "gene"), P(("grp", "cell"), None), P("gene"))
    return jax.shard_map(
        per_device,
        mesh=mesh,
        in_specs=placed,
        out_specs=(P(("grp", "cell"), "gene"), P(("grp", "gene", "cell"), None)),
        check_vma=False,
    )
```

profile of v0, /device:TPU:0, one launch (start us, length us, event | category | flops | bytes accessed | tf_op | source)
XLA Modules:
  0.0 335.5 jit_solution(2231902465308282045)
XLA Ops:
  7.2 0.7 copy-done
  7.9 0.8 fusion.18
  8.8 4.3 %fusion.17 = f32[8192,128]{1,0:T(8,128)} fusion(bf16[128,8192]{1,0:T(8,128)(2,1)} %param.3, bf16[128,128]{1,0:T(8,128)(2,1)S(1)} %copy-done), kind=kOutput, calls=%fused_computation.38 | convolution fusion | flops 268435456 | bytes 6324224 | tf_op jit(solution)/shard_map/dot_general | solution.py:40
  13.4 70.6 %all-reduce.3.cloned.1.call-done = f32[128,128]{0,1:T(8,128)} async-done(((f32[128,128]{0,1:T(8,128)}), f32[128,128]{0,1:T(8,128)}) %all-reduce.3.cloned.1.call-update) | async-done | bytes 65552 | tf_op jit(solution)/shard_map/psum | solution.py:47
  84.0 0.8 convert_add_fusion
  84.9 11.7 %cholesky.29 = f32[128,128]{1,0:T(8,128)S(1)} custom-call(f32[128,128]{1,0:T(8,128)S(1)} %fusion.13), custom_call_target="Cholesky" | custom-call | tf_op jit(solution)/shard_map/jit(cholesky)/cholesky | solution.py:17
  96.7 0.6 compare_reduce_fusion
  97.3 0.7 fusion.10
  98.0 9.8 %custom-call.6 = f32[1,128,128]{1,2,0:T(8,128)S(1)} custom-call(f32[1,128,128]{2,1,0:T(8,128)S(1)} %fusion.10), custom_call_target="InvertDiagBlocksLowerTriangular" | custom-call | tf_op jit(solution)/shard_map/triangular_solve | solution.py:18
  107.8 0.2 fusion.11
  108.0 0.3 fusion.19
  108.3 67.6 %reduce-scatter.2.cloned.1.call-done = f32[1024,128]{1,0:T(8,128)} async-done(((f32[8192,128]{1,0:T(8,128)}), f32[1024,128]{1,0:T(8,128)}) %reduce-scatter.2.cloned.1.call-update) | async-done | bytes 524304 | tf_op jit(solution)/shard_map/reduce_scatter | solution.py:39
  176.0 2.3 fusion.16
  178.3 1.6 fusion.20
  180.0 0.2 all-gather.2.cloned.1.call-start
  180.2 2.4 copy.5
  182.7 83.3 %all-reduce.5.cloned.1.call-done = f32[128,128]{1,0:T(8,128)} async-done(((f32[128,128]{1,0:T(8,128)}), f32[128,128]{1,0:T(8,128)}) %all-reduce.5.cloned.1.call-update) | async-done | bytes 65552 | tf_op jit(solution)/shard_map/psum | solution.py:53
  266.0 1.5 select_reduce_fusion
  267.5 1.7 fusion.9
  269.3 1.7 fusion.15
  271.0 0.2 fusion.8
  271.2 0.2 fusion.21
  271.7 0.2 fusion.7
  271.9 0.2 fusion.23
  272.7 0.2 fusion.26
  273.2 0.2 fusion.27
  273.4 0.2 fusion.28
  274.0 0.2 fusion.30
  275.3 1.4 fusion.1
  276.6 42.0 %all-gather.2.cloned.1.call-done = bf16[8192,128]{1,0:T(8,128)(2,1)} async-done(((bf16[1024,128]{1,0:T(8,128)(2,1)}), bf16[8192,128]{1,0:T(8,128)(2,1)}) %all-gather.2.cloned.1.call-update) | async-done | bytes 2097168 | tf_op jit(solution)/shard_map/all_gather | solution.py:59
  318.7 6.2 %subtract_convert_fusion = bf16[128,8192]{0,1:T(8,128)(2,1)} fusion(bf16[8192,128]{1,0:T(8,128)(2,1)} %all-gather.2.cloned.1.call-done, bf16[128,128]{1,0:T(8,128)(2,1)S(1)} %copy-done, bf16[128,8192]{0,1:T(8,128)(2,1)S(1)} %copy-done.2, f32[8192]{0:T(1024)S(1)} %broadcast_add_fusion, f32[8192]{0:T(1024)S(1)} %copy-done.3), kind=kOutput, calls=%fused_computation.2 | convolution fusion | flops 274726912 | bytes 6389760 | tf_op jit(solution)/shard_map/dot_general | solution.py:57
  324.9 4.1 %copy.9 = bf16[128,8192]{1,0:T(8,128)(2,1)} copy(bf16[128,8192]{0,1:T(8,128)(2,1)} %subtract_convert_fusion) | data formatting | bytes 4194304
  (33 shorter events, 3.1 us)
Async XLA Ops:
  7.2 0.8 copy-start
  7.2 76.8 %all-reduce.3.cloned.1.call-start = ((), (), s32[]{:S(2)}) async-start(), calls=%async_computation.2 | async-start | bytes 131072 | tf_op jit(solution)/shard_map/psum | solution.py:47
  8.8 167.2 %reduce-scatter.2.cloned.1.call-start = ((), (), s32[]{:S(2)}) async-start(), calls=%async_computation.1 | async-start | bytes 4718592 | tf_op jit(solution)/shard_map/reduce_scatter | solution.py:39
  13.1 167.0 %copy-start.3 = (f32[8192]{0:T(1024)S(1)}, f32[8192]{0:T(1024)}, u32[]{:S(2)}) copy-start(f32[8192]{0:T(1024)} %param.5) | copy-start | bytes 98308
  13.2 167.1 %copy-start.1 = (bf16[128,8192]{1,0:T(8,128)(2,1)S(1)}, bf16[128,8192]{1,0:T(8,128)(2,1)}, u32[]{:S(2)}) copy-start(bf16[128,8192]{1,0:T(8,128)(2,1)} %param.3) | copy-start | bytes 6291460
  13.2 252.8 %all-reduce.5.cloned.1.call-start = ((), (), s32[]{:S(2)}) async-start(), calls=%async_computation.4 | async-start | bytes 131072 | tf_op jit(solution)/shard_map/psum | solution.py:53
  180.0 138.7 %all-gather.2.cloned.1.call-start = ((), (), s32[]{:S(2)}) async-start(), calls=%async_computation.3 | async-start | bytes 2359296 | tf_op jit(solution)/shard_map/all_gather | solution.py:59
  271.9 46.8 %copy-start.2 = (bf16[128,8192]{0,1:T(8,128)(2,1)S(1)}, bf16[128,8192]{0,1:T(8,128)(2,1)}, u32[]{:S(2)}) copy-start(bf16[128,8192]{0,1:T(8,128)(2,1)} %copy.5) | copy-start | bytes 6291460
Sparse Core Ops, SparseCore 0:
  12.0 71.9 all-reduce.2
  87.6 88.3 reduce-scatter.1
  180.1 85.8 all-reduce.4
  268.0 50.6 all-gather.1
where the time goes:
time: 336 us; the launch traced here: 335 us
  waiting for transfers between devices  264 us (79%)
  other arithmetic  25.2 us (8%)
  matrix products  24.8 us (7%)
  between operations  14 us (4%)
  local copies, waits for them, and re-layouts  7.44 us (2%)
    psum x1, waiting for transfers between devices, per_device(): moment = lax.psum(local_moment, ('cell', 'gene'))  83.3 us
    psum x1, waiting for transfers between devices, per_device(): gram_total = lax.psum(local_gram, 'cell')  70.6 us
    reduce_scatter x1, waiting for transfers between devices, per_device(): lax.psum_scatter(lax.dot_general(expression, design, (((0,), (0,)), ((),...  67.6 us
    all_gather x1, waiting for transfers between devices, per_device(): lax.all_gather(coef_low, 'cell', axis=0, tiled=True)  42 us
    another operation x4, other arithmetic, invert(): factor = jnp.linalg.cholesky(matrix)  12.4 us
    dot_general x26, matrix products, matmul(): return jnp.dot(left, right, precision=lax.Precision.HIGHEST)  11.6 us
    another operation x2, other arithmetic, invert(): lax.linalg.triangular_solve(factor, identity, left_side=True, lower=True)  10.5 us
    unnamed x10, local copies, waits for them, and re-layouts  7.23 us
  transfers between devices with their start and end apart: 4, of which 4 were waited for; matrix products, arithmetic and copies ran while one was open for 12% of the time, Pallas kernels for 0%

commit v1 on v0

--- a/solution.py
+++ b/solution.py
@@ -6,6 +6,18 @@
 
 NS_STEPS = 8
 shrink_rate = 0.25
+
+
+def collect(array, axis, dim):
+    ways, here, step = (lax.axis_size(axis), lax.axis_index(axis), array.shape[dim])
+    line, have = (array, 1)
+    while have < ways:
+        line = jnp.concatenate(
+            [line, lax.ppermute(line, axis, [(d, (d - have) % ways) for d in range(ways)])],
+            axis=dim,
+        )
+        have = 2 * have
+    return jnp.roll(line, here * step, axis=dim)
 
 
 def matmul(left, right):
@@ -56,7 +68,7 @@
     coef_low = coef.astype(jnp.bfloat16)
     fitted = lax.dot_general(
         design,
-        lax.all_gather(coef_low, "cell", axis=0, tiled=True),
+        collect(coef_low, "cell", 0),
         (((1,), (1,)), ((), ())),
         preferred_element_type=jnp.float32,
     )

time: 336 us -> 350 us (1.042)
  starting transfers between devices: 0.34 us -> 10.7 us
  waiting for transfers between devices: 264 us -> 269 us
    ppermute x0 -> x3, waiting for transfers between devices: none -> 49.6 us  [collect(): lax.ppermute(line, axis, [(d, (d - have) % ways) for d in range(ways)])]
    all_gather x1 -> x0, waiting for transfers between devices: 42 us -> none  [per_device(): lax.all_gather(coef_low, 'cell', axis=0, tiled=True)]
    ppermute x0 -> x3, starting transfers between devices: none -> 10.6 us  [collect(): lax.ppermute(line, axis, [(d, (d - have) % ways) for d in range(ways)])]
    unnamed x10 -> x18, local copies, waits for them, and re-layouts: 7.23 us -> 6.44 us
  transfers between devices with their start and end apart: 4 -> 6, of which waited for: 4 -> 5; matrix products, arithmetic and copies ran while one was open for 12% -> 12% of each run, Pallas kernels for 0% -> 0%
where the time goes in v1:
time: 350 us
  waiting for transfers between devices  269 us (77%)
  other arithmetic  25.3 us (7%)
  matrix products  23.9 us (7%)
  between operations  14.1 us (4%)
  starting transfers between devices  10.7 us (3%)
  local copies, waits for them, and re-layouts  6.78 us (2%)
    psum x1, waiting for transfers between devices, per_device(): moment = lax.psum(local_moment, ('cell', 'gene'))  81.3 us
    psum x1, waiting for transfers between devices, per_device(): gram_total = lax.psum(local_gram, 'cell')  70.6 us
    reduce_scatter x1, waiting for transfers between devices, per_device(): lax.psum_scatter(lax.dot_general(expression, design, (((0,), (0,)), ((),...  67.6 us
    ppermute x3, waiting for transfers between devices, collect(): lax.ppermute(line, axis, [(d, (d - have) % ways) for d in range(ways)])  49.6 us
    another operation x4, other arithmetic, invert(): factor = jnp.linalg.cholesky(matrix)  12.4 us
    dot_general x26, matrix products, matmul(): return jnp.dot(left, right, precision=lax.Precision.HIGHEST)  11.9 us
    ppermute x3, starting transfers between devices, collect(): lax.ppermute(line, axis, [(d, (d - have) % ways) for d in range(ways)])  10.6 us
    another operation x2, other arithmetic, invert(): lax.linalg.triangular_solve(factor, identity, left_side=True, lower=True)  10.5 us
  transfers between devices with their start and end apart: 6, of which 5 were waited for; matrix products, arithmetic and copies ran while one was open for 12% of the time, Pallas kernels for 0%

profile of v1, /device:TPU:0, one launch (start us, length us, event | category | flops | bytes accessed | tf_op | source)
XLA Modules:
  0.0 350.0 jit_solution(6389962338625508100)
XLA Ops:
  7.2 0.7 copy-done
  7.9 0.8 fusion.19
  8.8 4.3 %fusion.18 = f32[8192,128]{1,0:T(8,128)} fusion(bf16[128,8192]{1,0:T(8,128)(2,1)} %param.3, bf16[128,128]{1,0:T(8,128)(2,1)S(1)} %copy-done), kind=kOutput, calls=%fused_computation.49 | convolution fusion | flops 268435456 | bytes 6324224 | tf_op jit(solution)/shard_map/dot_general | solution.py:52
  13.3 70.6 %all-reduce.3.cloned.1.call-done = f32[128,128]{0,1:T(8,128)} async-done(((f32[128,128]{0,1:T(8,128)}), f32[128,128]{0,1:T(8,128)}) %all-reduce.3.cloned.1.call-update) | async-done | bytes 65552 | tf_op jit(solution)/shard_map/psum | solution.py:59
  84.0 0.8 convert_add_fusion
  84.9 11.7 %cholesky.29 = f32[128,128]{1,0:T(8,128)S(1)} custom-call(f32[128,128]{1,0:T(8,128)S(1)} %fusion.14), custom_call_target="Cholesky" | custom-call | tf_op jit(solution)/shard_map/jit(cholesky)/cholesky | solution.py:29
  96.7 0.6 compare_reduce_fusion
  97.3 0.7 fusion.11
  98.0 9.8 %custom-call.6 = f32[1,128,128]{1,2,0:T(8,128)S(1)} custom-call(f32[1,128,128]{2,1,0:T(8,128)S(1)} %fusion.11), custom_call_target="InvertDiagBlocksLowerTriangular" | custom-call | tf_op jit(solution)/shard_map/triangular_solve | solution.py:30
  107.8 0.2 fusion.12
  108.0 0.3 fusion.20
  108.3 67.6 %reduce-scatter.2.cloned.1.call-done = f32[1024,128]{1,0:T(8,128)} async-done(((f32[8192,128]{1,0:T(8,128)}), f32[1024,128]{1,0:T(8,128)}) %reduce-scatter.2.cloned.1.call-update) | async-done | bytes 524304 | tf_op jit(solution)/shard_map/reduce_scatter | solution.py:51
  175.9 2.3 constant_dynamic-update-slice_fusion.7
  178.2 1.6 fusion.21
  179.9 2.4 copy.5
  182.4 3.0 collective-permute-start
  185.3 81.3 %all-reduce.5.cloned.1.call-done = f32[128,128]{1,0:T(8,128)} async-done(((f32[128,128]{1,0:T(8,128)}), f32[128,128]{1,0:T(8,128)}) %all-reduce.5.cloned.1.call-update) | async-done | bytes 65552 | tf_op jit(solution)/shard_map/psum | solution.py:65
  266.7 1.5 select_reduce_fusion
  268.1 1.7 fusion.10
  270.0 2.0 fusion.16
  272.0 0.2 fusion.9
  272.7 0.2 fusion.8
  273.3 0.2 fusion.7
  273.9 0.2 fusion.6
  274.6 0.2 fusion.5
  275.3 5.1 %collective-permute-start.1 = (bf16[2048,128]{1,0:T(8,128)(2,1)S(1)}, bf16[2048,128]{1,0:T(8,128)(2,1)S(1)}, u32[]{:S(2)}, u32[]{:S(2)}) collective-permute-start(bf16[2048,128]{1,0:T(8,128)(2,1)S(1)} %pad_maximum_fusion.1), channel_id=1, source_target_pairs={{0,12},{2,14},{4,0},{6,2},{8,4},{10,6},{12,8},{14,10},{1,13},{3,15... | collective-permute-start | bytes 1572872 | tf_op jit(solution)/shard_map/ppermute | solution.py:16
  281.0 8.4 %collective-permute-done.1 = bf16[2048,128]{1,0:T(8,128)(2,1)S(1)} collective-permute-done((bf16[2048,128]{1,0:T(8,128)(2,1)S(1)}, bf16[2048,128]{1,0:T(8,128)(2,1)S(1)}, u32[]{:S(2)}, u32[]{:S(2)}) %collective-permute-start.1) | collective-permute-done | bytes 524320 | tf_op jit(solution)/shard_map/ppermute | solution.py:16
  289.5 2.6 collective-permute-start.2
  292.5 1.4 fusion.2
  294.0 41.1 %collective-permute-done.2 = bf16[4096,128]{1,0:T(8,128)(2,1)S(1)} collective-permute-done((bf16[4096,128]{1,0:T(8,128)(2,1)S(1)}, bf16[4096,128]{1,0:T(8,128)(2,1)S(1)}, u32[]{:S(2)}, u32[]{:S(2)}) %collective-permute-start.2) | collective-permute-done | bytes 1048608 | tf_op jit(solution)/shard_map/ppermute | solution.py:16
  335.5 5.0 %subtract_convert_fusion = bf16[128,8192]{0,1:T(8,128)(2,1)S(1)} fusion(bf16[128,128]{1,0:T(8,128)(2,1)S(1)} %copy-done, bf16[128,8192]{0,1:T(8,128)(2,1)S(1)} %copy-done.2, f32[8192]{0:T(1024)S(1)} %broadcast_add_fusion, f32[8192]{0:T(1024)S(1)} %copy-done.3, bf16[16384,128]{1,0:T(8,128)(2,1)S(1)} %constant_dynamic-update-slice_fusion, s32[]{:T(128)S(6)} %select_n.24), kind=kOutput, calls=%fused_computation.2 | convolution fusion | flops 274726912 | bytes 6389764 | tf_op jit(solution)/shard_map/dot_general | solution.py:69
  340.6 2.9 copy.9
  (47 shorter events, 4.3 us)
Async XLA Ops:
  7.2 0.8 copy-start
  7.2 76.8 %all-reduce.3.cloned.1.call-start = ((), (), s32[]{:S(2)}) async-start(), calls=%async_computation.2 | async-start | bytes 131072 | tf_op jit(solution)/shard_map/psum | solution.py:59
  8.8 167.1 %reduce-scatter.2.cloned.1.call-start = ((), (), s32[]{:S(2)}) async-start(), calls=%async_computation.1 | async-start | bytes 4718592 | tf_op jit(solution)/shard_map/reduce_scatter | solution.py:51
  13.1 166.8 %copy-start.3 = (f32[8192]{0:T(1024)S(1)}, f32[8192]{0:T(1024)}, u32[]{:S(2)}) copy-start(f32[8192]{0:T(1024)} %param.5) | copy-start | bytes 98308
  13.1 166.8 %copy-start.1 = (bf16[128,8192]{1,0:T(8,128)(2,1)S(1)}, bf16[128,8192]{1,0:T(8,128)(2,1)}, u32[]{:S(2)}) copy-start(bf16[128,8192]{1,0:T(8,128)(2,1)} %param.3) | copy-start | bytes 6291460
  13.2 253.5 %all-reduce.5.cloned.1.call-start = ((), (), s32[]{:S(2)}) async-start(), calls=%async_computation.3 | async-start | bytes 131072 | tf_op jit(solution)/shard_map/psum | solution.py:65
  182.4 92.8 %collective-permute-start = (bf16[1024,128]{1,0:T(8,128)(2,1)S(1)}, bf16[1024,128]{1,0:T(8,128)(2,1)S(1)}, u32[]{:S(2)}, u32[]{:S(2)}) collective-permute-start(bf16[1024,128]{1,0:T(8,128)(2,1)S(1)} %get-tuple-element.5), channel_id=1, source_target_pairs={{0,14},{2,0},{4,2},{6,4},{8,6},{10,8},{12,10},{14,12},{1,15},{3,1}... | collective-permute-start | bytes 786440 | tf_op jit(solution)/shard_map/ppermute | solution.py:16
  270.0 23.8 %copy-start.4 = (bf16[16384,128]{1,0:T(8,128)(2,1)S(1)}, bf16[16384,128]{1,0:T(8,128)(2,1)}, u32[]{:S(2)}) copy-start(bf16[16384,128]{1,0:T(8,128)(2,1)} %get-tuple-element.4) | copy-start | bytes 12582916
  275.3 14.2 %collective-permute-start.1 = (bf16[2048,128]{1,0:T(8,128)(2,1)S(1)}, bf16[2048,128]{1,0:T(8,128)(2,1)S(1)}, u32[]{:S(2)}, u32[]{:S(2)}) collective-permute-start(bf16[2048,128]{1,0:T(8,128)(2,1)S(1)} %pad_maximum_fusion.1), channel_id=1, source_target_pairs={{0,12},{2,14},{4,0},{6,2},{8,4},{10,6},{12,8},{14,10},{1,13},{3,15... | collective-permute-start | bytes 1572872 | tf_op jit(solution)/shard_map/ppermute | solution.py:16
  289.5 45.6 %collective-permute-start.2 = (bf16[4096,128]{1,0:T(8,128)(2,1)S(1)}, bf16[4096,128]{1,0:T(8,128)(2,1)S(1)}, u32[]{:S(2)}, u32[]{:S(2)}) collective-permute-start(bf16[4096,128]{1,0:T(8,128)(2,1)S(1)} %pad_maximum_fusion), channel_id=1, source_target_pairs={{0,8},{2,10},{4,12},{6,14},{8,0},{10,2},{12,4},{14,6},{1,9},{3,11}... | collective-permute-start | bytes 3145736 | tf_op jit(solution)/shard_map/ppermute | solution.py:16
  293.8 41.7 %copy-start.2 = (bf16[128,8192]{0,1:T(8,128)(2,1)S(1)}, bf16[128,8192]{0,1:T(8,128)(2,1)}, u32[]{:S(2)}) copy-start(bf16[128,8192]{0,1:T(8,128)(2,1)} %copy.5) | copy-start | bytes 6291460
Sparse Core Ops, SparseCore 0:
  12.0 71.9 all-reduce.2
  87.6 88.2 reduce-scatter.1
  180.0 86.6 all-reduce.4

commit v2 on v0

--- a/solution.py
+++ b/solution.py
@@ -50,7 +50,7 @@
     local_moment = lax.dot_general(
         coef, coef, (((0,), (0,)), ((), ())), precision=lax.Precision.HIGHEST
     )
-    moment = lax.psum(local_moment, ("cell", "gene"))
+    moment = jnp.sum(lax.all_gather(local_moment, ("cell", "gene")), axis=0)
     root_inv = newton(moment)
     low_rank_coef = coef - shrink_rate / math.sqrt(width) * matmul(coef, root_inv)
     coef_low = coef.astype(jnp.bfloat16)

time: 336 us -> 285 us (0.85)
  waiting for transfers between devices: 264 us -> 214 us
    psum x1 -> x0, waiting for transfers between devices: 83.3 us -> none  [per_device(): moment = lax.psum(local_moment, ('cell', 'gene'))]
    all_gather x0 -> x1, waiting for transfers between devices: none -> 34.9 us  [per_device(): moment = jnp.sum(lax.all_gather(local_moment, ('cell', 'gene')), axis=0)]
  transfers between devices with their start and end apart: 4 -> 4, of which waited for: 4 -> 4; matrix products, arithmetic and copies ran while one was open for 12% -> 14% of each run, Pallas kernels for 0% -> 0%
where the time goes in v2:
time: 285 us
  waiting for transfers between devices  214 us (75%)
  other arithmetic  25.6 us (9%)
  matrix products  23.1 us (8%)
  between operations  14 us (5%)
  local copies, waits for them, and re-layouts  7.44 us (3%)
    psum x1, waiting for transfers between devices, per_device(): gram_total = lax.psum(local_gram, 'cell')  70.6 us
    reduce_scatter x1, waiting for transfers between devices, per_device(): lax.psum_scatter(lax.dot_general(expression, design, (((0,), (0,)), ((),...  67.6 us
    all_gather x1, waiting for transfers between devices, per_device(): lax.all_gather(coef_low, 'cell', axis=0, tiled=True)  40.8 us
    all_gather x1, waiting for transfers between devices, per_device(): moment = jnp.sum(lax.all_gather(local_moment, ('cell', 'gene')), axis=0)  34.9 us
    another operation x4, other arithmetic, invert(): factor = jnp.linalg.cholesky(matrix)  12.4 us
    another operation x2, other arithmetic, invert(): lax.linalg.triangular_solve(factor, identity, left_side=True, lower=True)  10.5 us
    dot_general x26, matrix products, matmul(): return jnp.dot(left, right, precision=lax.Precision.HIGHEST)  9.95 us
    unnamed x10, local copies, waits for them, and re-layouts  7.23 us
  transfers between devices with their start and end apart: 4, of which 4 were waited for; matrix products, arithmetic and copies ran while one was open for 14% of the time, Pallas kernels for 0%

profile of v2, /device:TPU:0, one launch (start us, length us, event | category | flops | bytes accessed | tf_op | source)
XLA Modules:
  0.0 284.5 jit_solution(5698593669830499091)
XLA Ops:
  7.2 0.7 copy-done
  7.9 0.8 fusion.18
  8.8 4.3 %fusion.17 = f32[8192,128]{1,0:T(8,128)} fusion(bf16[128,8192]{1,0:T(8,128)(2,1)} %param.3, bf16[128,128]{1,0:T(8,128)(2,1)S(1)} %copy-done), kind=kOutput, calls=%fused_computation.38 | convolution fusion | flops 268435456 | bytes 6324224 | tf_op jit(solution)/shard_map/dot_general | solution.py:40
  13.3 70.6 %all-reduce.2.cloned.1.call-done = f32[128,128]{0,1:T(8,128)} async-done(((f32[128,128]{0,1:T(8,128)}), f32[128,128]{0,1:T(8,128)}) %all-reduce.2.cloned.1.call-update) | async-done | bytes 65552 | tf_op jit(solution)/shard_map/psum | solution.py:47
  84.0 0.8 convert_add_fusion
  84.9 11.7 %cholesky.29 = f32[128,128]{1,0:T(8,128)S(1)} custom-call(f32[128,128]{1,0:T(8,128)S(1)} %fusion.13), custom_call_target="Cholesky" | custom-call | tf_op jit(solution)/shard_map/jit(cholesky)/cholesky | solution.py:17
  96.7 0.6 compare_reduce_fusion
  97.3 0.7 fusion.10
  98.0 9.8 %custom-call.6 = f32[1,128,128]{1,2,0:T(8,128)S(1)} custom-call(f32[1,128,128]{2,1,0:T(8,128)S(1)} %fusion.10), custom_call_target="InvertDiagBlocksLowerTriangular" | custom-call | tf_op jit(solution)/shard_map/triangular_solve | solution.py:18
  107.8 0.2 fusion.11
  108.0 0.3 fusion.19
  108.3 67.6 %reduce-scatter.2.cloned.1.call-done = f32[1024,128]{1,0:T(8,128)} async-done(((f32[8192,128]{1,0:T(8,128)}), f32[1024,128]{1,0:T(8,128)}) %reduce-scatter.2.cloned.1.call-update) | async-done | bytes 524304 | tf_op jit(solution)/shard_map/reduce_scatter | solution.py:39
  176.0 2.3 fusion.16
  178.3 1.6 fusion.20
  180.0 0.2 all-gather.4.cloned.1.call-start
  180.2 2.4 copy.5
  182.7 34.9 %all-gather.6.cloned.1.call-done = f32[2048,128]{1,0:T(8,128)} async-done(((f32[128,128]{1,0:T(8,128)}), f32[2048,128]{1,0:T(8,128)}) %all-gather.6.cloned.1.call-update) | async-done | bytes 1048592 | tf_op jit(solution)/shard_map/all_gather | solution.py:53
  217.6 1.3 reduce_sum.19
  218.9 0.6 select_reduce_fusion
  219.5 0.8 fusion.9
  220.5 0.8 fusion.15
  221.4 0.2 fusion.8
  221.6 0.2 fusion.21
  222.0 0.2 fusion.7
  222.2 0.2 fusion.23
  222.4 0.2 fusion.24
  222.7 0.2 fusion.6
  223.3 0.2 fusion.5
  225.6 1.4 fusion.1
  227.0 40.8 %all-gather.4.cloned.1.call-done = bf16[8192,128]{1,0:T(8,128)(2,1)} async-done(((bf16[1024,128]{1,0:T(8,128)(2,1)}), bf16[8192,128]{1,0:T(8,128)(2,1)}) %all-gather.4.cloned.1.call-update) | async-done | bytes 2097168 | tf_op jit(solution)/shard_map/all_gather | solution.py:59
  267.8 6.2 %subtract_convert_fusion = bf16[128,8192]{0,1:T(8,128)(2,1)} fusion(bf16[8192,128]{1,0:T(8,128)(2,1)} %all-gather.4.cloned.1.call-done, bf16[128,128]{1,0:T(8,128)(2,1)S(1)} %copy-done, bf16[128,8192]{0,1:T(8,128)(2,1)S(1)} %copy-done.2, f32[8192]{0:T(1024)S(1)} %broadcast_add_fusion, f32[8192]{0:T(1024)S(1)} %copy-done.3), kind=kOutput, calls=%fused_computation.2 | convolution fusion | flops 274726912 | bytes 6389760 | tf_op jit(solution)/shard_map/dot_general | solution.py:57
  273.9 4.1 %copy.9 = bf16[128,8192]{1,0:T(8,128)(2,1)} copy(bf16[128,8192]{0,1:T(8,128)(2,1)} %subtract_convert_fusion) | data formatting | bytes 4194304
  (34 shorter events, 3.3 us)
Async XLA Ops:
  7.2 0.8 copy-start
  7.2 76.8 %all-reduce.2.cloned.1.call-start = ((), (), s32[]{:S(2)}) async-start(), calls=%async_computation.2 | async-start | bytes 131072 | tf_op jit(solution)/shard_map/psum | solution.py:47
  8.8 167.2 %reduce-scatter.2.cloned.1.call-start = ((), (), s32[]{:S(2)}) async-start(), calls=%async_computation.1 | async-start | bytes 4718592 | tf_op jit(solution)/shard_map/reduce_scatter | solution.py:39
  13.1 167.1 %copy-start.1 = (bf16[128,8192]{1,0:T(8,128)(2,1)S(1)}, bf16[128,8192]{1,0:T(8,128)(2,1)}, u32[]{:S(2)}) copy-start(bf16[128,8192]{1,0:T(8,128)(2,1)} %param.3) | copy-start | bytes 6291460
  13.2 204.4 %all-gather.6.cloned.1.call-start = ((), (), s32[]{:S(2)}) async-start(), calls=%async_computation.4 | async-start | bytes 1114112 | tf_op jit(solution)/shard_map/all_gather | solution.py:53
  179.9 2.7 copy-start.3
  180.0 87.8 %all-gather.4.cloned.1.call-start = ((), (), s32[]{:S(2)}) async-start(), calls=%async_computation.3 | async-start | bytes 2359296 | tf_op jit(solution)/shard_map/all_gather | solution.py:59
  222.2 45.5 %copy-start.2 = (bf16[128,8192]{0,1:T(8,128)(2,1)S(1)}, bf16[128,8192]{0,1:T(8,128)(2,1)}, u32[]{:S(2)}) copy-start(bf16[128,8192]{0,1:T(8,128)(2,1)} %copy.5) | copy-start | bytes 6291460
Sparse Core Ops, SparseCore 0:
  12.0 71.9 all-reduce.1
  87.6 88.3 reduce-scatter.1
  180.1 37.4 all-gather.5
  219.6 48.1 all-gather.3
